TPU v7x, 32 devices: a whole 2x2x4 slice. The times are simulated.
32 devices in a mesh: groups: 2 (over y), tensor: 4 (over x, core), dp: 4 (over z).
Axes of the slice: x: 2, y: 2, z: 4, core: 2. Of those that a mesh axis runs over, the one named last changes fastest.
Arguments:
- tokens: bfloat16 [65536, 4096], P(('groups', 'dp'), 'tensor'), parts along dimension 0, may hold values from -6 to 6
- cotangent: bfloat16 [65536, 4096], P(('groups', 'dp'), 'tensor'), parts along dimension 0, may hold values from -6 to 6
- w_first: bfloat16 [16, 256, 256], P('tensor'), may hold values from -0.375 to 0.375
- w_second: bfloat16 [16, 256, 256], P('tensor'), may hold values from -0.375 to 0.375
Outputs:
- grad_tokens: bfloat16 [65536, 4096], P(('groups', 'dp'), 'tensor'), parts along dimension 0
- grad_first: float32 [32, 256, 256], P(('groups', 'tensor'), 'dp'), parts along dimension 0
- grad_second: float32 [32, 256, 256], P(('groups', 'tensor'), 'dp'), parts along dimension 0
There are 2 independent parts, one for each index of `groups`. A program takes and returns all parts, laid end to end along the dimension named above; an argument that names none is the same for every part. Nothing has to cross between parts.
All inputs are finite; a program needn't handle non-finite values.
Results may differ from a plain program's by a relative error of at most 0.0065.
Values may be sent and summed in bfloat16 or wider, within the bound.
No kernel may reach another device: no remote copies, remote signals or barrier semaphores. Data moves between devices by JAX's collectives and lax.ppermute only.
A program may use at most 192 MiB of HBM per device.

v0:
```python
import math
import jax
import jax.numpy as jnp
from jax import lax
from jax.sharding import PartitionSpec as P

NB = 16


def shards(tokens, cotangent, w_first, w_second):
    tok_rows = tokens.shape[0]
    blk_local = w_first.shape[0]
    blk_width = w_first.shape[1]
    sub_width = blk_width // NB
    dp_count = lax.axis_size("dp")
    grad_scale = 1.0 / math.sqrt(tok_rows * dp_count)
    inputs = tokens.reshape(tok_rows, blk_local, blk_width)
    upstream = cotangent.reshape(tok_rows, blk_local, blk_width)
    hidden = jnp.einsum("tbi,bij->bjt", inputs, w_first, preferred_element_type=jnp.float32).astype(
        jnp.bfloat16
    )
    hidden = hidden.reshape(blk_local, NB, sub_width, tok_rows)
    second_view = w_second.reshape(blk_local, sub_width, NB, blk_width)
    moved = lax.all_to_all(hidden, "tensor", split_axis=1, concat_axis=0, tiled=True)
    active = jnp.maximum(moved, jnp.zeros((), jnp.bfloat16))
    second_term = jnp.einsum("bcjt,tco->cjbo", active, upstream, preferred_element_type=jnp.float32)
    second_term = second_term.reshape(blk_local, blk_width, blk_width) * grad_scale
    backed = jnp.einsum("tco,cjbo->bcjt", upstream, second_view, preferred_element_type=jnp.float32)
    masked = jnp.where(moved > 0, backed, jnp.zeros((), jnp.float32)).astype(jnp.bfloat16)
    returned = lax.all_to_all(masked, "tensor", split_axis=0, concat_axis=1, tiled=True)
    returned = returned.reshape(blk_local, blk_width, tok_rows)
    first_term = (
        jnp.einsum("tbi,bjt->bij", inputs, returned, preferred_element_type=jnp.float32)
        * grad_scale
    )
    grad_tokens = jnp.einsum("bjt,bij->tbi", returned, w_first, preferred_element_type=jnp.float32)
    grad_tokens = grad_tokens.astype(jnp.bfloat16).reshape(tok_rows, blk_local * blk_width)
    grad_first, grad_second = (
        lax.psum_scatter(first_term, "dp", scatter_dimension=1, tiled=True),
        lax.psum_scatter(second_term, "dp", scatter_dimension=1, tiled=True),
    )
    return (grad_tokens, grad_first, grad_second)


def solution(mesh):
    return jax.shard_map(
        shards,
        mesh=mesh,
        in_specs=(
            P(("groups", "dp"), "tensor"),
            P(("groups", "dp"), "tensor"),
            P("tensor", None, None),
            P("tensor", None, None),
        ),
        out_specs=(
            P(("groups", "dp"), "tensor"),
            P(("groups", "tensor"), "dp", None),
            P(("groups", "tensor"), "dp", None),
        ),
        check_vma=False,
    )
```

profile of v0, /device:TPU:0, one launch (start us, length us, event | category | flops | bytes accessed | tf_op | source)
XLA Modules:
  0.0 638.0 jit_solution(12787721479795042683)
XLA Ops:
  7.2 0.0 copy-start
  7.2 1.0 copy-done
  8.2 20.5 %fusion.5 = bf16[4,256,8192]{2,1,0:T(8,128)(2,1)} fusion(bf16[4,256,256]{2,1,0:T(8,128)(2,1)S(1)} %copy-done, bf16[1024,4,8,256]{3,2,1,0:T(8,128)(2,1)} %bitcast.56), kind=kOutput, calls=%fused_computation.7 | convolution fusion | flops 4303355904 | bytes 34078720 | tf_op jit(solution)/shard_map/tbi,bij->bjt/dot_general | solution.py:19
  28.8 13.9 %copy.30 = bf16[4,16,16,8192]{3,2,0,1:T(8,128)(2,1)} copy(bf16[4,16,16,8192]{3,2,1,0:T(8,128)(2,1)} %bitcast.53) | data formatting | bytes 33554432 | tf_op jit(solution)/shard_map/reshape | solution.py:22
  42.6 7.0 %all-to-all-start = ((bf16[4,16,16,8192]{3,2,0,1:T(8,128)(2,1)}), bf16[4,16,16,8192]{3,2,0,1:T(8,128)(2,1)}, u32[]{:S(2)}, u32[]{:S(2)}) async-start(bf16[4,16,16,8192]{3,2,0,1:T(8,128)(2,1)} %copy.30), calls=%async_computation | async-start | bytes 33554432 | tf_op jit(solution)/shard_map/all_to_all | solution.py:24
  49.6 27.9 %reshape.39 = bf16[8192,4,256]{2,1,0:T(4,128)(2,1)} reshape(bf16[8192,1024]{1,0:T(8,128)(2,1)} %param.5) | data formatting | bytes 33554432 | tf_op jit(solution)/shard_map/reshape | solution.py:18
  77.5 155.8 %all-to-all-done = bf16[4,16,16,8192]{3,2,0,1:T(8,128)(2,1)} async-done(((bf16[4,16,16,8192]{3,2,0,1:T(8,128)(2,1)}), bf16[4,16,16,8192]{3,2,0,1:T(8,128)(2,1)}, u32[]{:S(2)}, u32[]{:S(2)}) %all-to-all-start) | async-done | bytes 16777248 | tf_op jit(solution)/shard_map/all_to_all | solution.py:24
  233.3 7.4 %broadcast_compare_fusion = pred[4,16,16,8192]{3,2,0,1:T(8,128)(4,1)S(1)} fusion(bf16[4,16,16,8192]{3,2,0,1:T(8,128)(2,1)} %all-to-all-done), kind=kLoop, calls=%fused_computation.15 | loop fusion | flops 8388608 | bytes 25165824 | tf_op jit(solution)/shard_map/gt | solution.py:29
  240.7 25.3 %copy.71 = pred[4,4,4,16,8192]{4,0,1,3,2:T(4,128)(4,1)} copy(pred[4,4,4,16,8192]{4,3,0,2,1:T(8,128)(4,1)S(1)} %bitcast.54) | data formatting | bytes 16777216 | tf_op jit(solution)/shard_map/gt | solution.py:29
  265.9 20.9 %gt.15 = pred[16,4,16,8192]{3,0,2,1:T(8,128)(4,1)} reshape(pred[4,4,4,16,8192]{4,1,0,3,2:T(4,128)(4,1)} %bitcast.55) | data formatting | bytes 16777216 | tf_op jit(solution)/shard_map/gt | solution.py:29
  286.8 24.9 %fusion = bf16[16,4,16,8192]{3,0,2,1:T(8,128)(2,1)} fusion(pred[16,4,16,8192]{3,0,2,1:T(8,128)(4,1)} %gt.15, bf16[4,16,16,256]{3,2,1,0:T(8,128)(2,1)S(1)} %bitcast.62, bf16[8192,4,256,1]{2,1,0,3:T(4,128)(2,1)} %bitcast.58), kind=kOutput, calls=%fused_computation.1 | convolution fusion | flops 4311744512 | bytes 42467328 | tf_op jit(solution)/shard_map/tco,cjbo->bcjt/dot_general | solution.py:28
  311.7 18.5 %copy.33 = bf16[16,4,16,8192]{3,2,1,0:T(8,128)(2,1)} copy(bf16[16,4,16,8192]{3,0,2,1:T(8,128)(2,1)} %fusion) | data formatting | bytes 33554432 | tf_op jit(solution)/shard_map/convert_element_type | solution.py:29
  330.1 7.1 %all-to-all-start.1 = ((bf16[16,4,16,8192]{3,2,1,0:T(8,128)(2,1)}), bf16[16,4,16,8192]{3,2,1,0:T(8,128)(2,1)}, u32[]{:S(2)}, u32[]{:S(2)}) async-start(bf16[16,4,16,8192]{3,2,1,0:T(8,128)(2,1)} %copy.33), calls=%async_computation.1 | async-start | bytes 33554432 | tf_op jit(solution)/shard_map/all_to_all | solution.py:30
  337.2 0.2 all-reduce.3.cloned.1.call-start
  337.5 8.0 %broadcast_maximum_fusion = bf16[4,16,16,8192]{3,2,0,1:T(8,128)(2,1)S(1)} fusion(bf16[4,16,16,8192]{3,2,0,1:T(8,128)(2,1)} %all-to-all-done), kind=kLoop, calls=%fused_computation.14 | loop fusion | flops 8388608 | bytes 33554432 | tf_op jit(solution)/shard_map/max | solution.py:25
  345.4 6.6 %copy.37 = bf16[4,4,4,16,8192]{4,3,0,1,2:T(8,128)(2,1)} copy(bf16[4,4,4,16,8192]{4,3,0,2,1:T(8,128)(2,1)S(1)} %bitcast.51) | data formatting | bytes 33554432 | tf_op jit(solution)/shard_map/max | solution.py:25
  352.0 168.3 %all-to-all-done.1 = bf16[16,4,16,8192]{3,2,1,0:T(8,128)(2,1)} async-done(((bf16[16,4,16,8192]{3,2,1,0:T(8,128)(2,1)}), bf16[16,4,16,8192]{3,2,1,0:T(8,128)(2,1)}, u32[]{:S(2)}, u32[]{:S(2)}) %all-to-all-start.1) | async-done | bytes 16777248 | tf_op jit(solution)/shard_map/all_to_all | solution.py:30
  520.3 13.9 %copy.34 = bf16[4,4,4,16,8192]{4,3,2,0,1:T(8,128)(2,1)} copy(bf16[4,4,4,16,8192]{4,3,2,1,0:T(8,128)(2,1)} %bitcast.6) | data formatting | bytes 33554432 | tf_op jit(solution)/shard_map/all_to_all | solution.py:30
  534.2 12.9 %fusion.22 = f32[4,256,256]{1,2,0:T(8,128)S(1)} fusion(bf16[4,256,8192]{2,1,0:T(8,128)(2,1)} %bitcast.49, bf16[1024,4,8,256]{3,2,1,0:T(8,128)(2,1)} %bitcast.57), kind=kOutput, calls=%fused_computation.19 | convolution fusion | flops 4295229440 | bytes 34603008 | tf_op jit(solution)/shard_map/tbi,bjt->bij/dot_general | solution.py:33
  547.1 1.4 copy.36
  548.5 0.0 all-reduce.3.cloned.1.call-update
  548.5 0.0 reduce-scatter.2.cloned.1.call-start
  548.6 13.1 %fusion.16 = f32[4,16,16,256]{3,1,2,0:T(8,128)S(1)} fusion(bf16[16,4,16,8192]{3,2,0,1:T(8,128)(2,1)} %bitcast.60, bf16[8192,4,256,1]{2,1,0,3:T(4,128)(2,1)} %bitcast.59), kind=kOutput, calls=%fused_computation.17 | convolution fusion | flops 4295229440 | bytes 34603008 | tf_op jit(solution)/shard_map/bcjt,tco->cjbo/dot_general | solution.py:26
  561.7 1.6 copy.39
  563.3 0.0 reduce-scatter.2.cloned.1.call-update
  563.4 0.6 dynamic-slice
  564.6 13.9 %convolution_convert_fusion = bf16[4,8192,256]{1,2,0:T(8,128)(2,1)} fusion(bf16[4,256,256]{2,1,0:T(8,128)(2,1)S(1)} %copy-done, bf16[4,256,8192]{2,1,0:T(8,128)(2,1)} %bitcast.50), kind=kOutput, calls=%fused_computation.8 | convolution fusion | flops 4303355904 | bytes 34078720 | tf_op jit(solution)/shard_map/bjt,bij->tbi/dot_general | solution.py:36
  578.5 22.5 %copy.40 = bf16[8192,1024]{1,0:T(8,128)(2,1)} copy(bf16[8192,1024]{0,1:T(8,128)(2,1)} %bitcast.52) | data formatting | bytes 33554432
  601.0 0.7 all-reduce.3.cloned.1.call-done
  601.7 1.0 constant_dynamic-slice_fusion
  602.6 0.8 copy.41
  603.4 27.8 %reduce-scatter.2.cloned.1.call-done = f32[4,64,256]{2,1,0:T(8,128)} async-done(((f32[4,256,256]{2,1,0:T(8,128)}), f32[4,64,256]{2,1,0:T(8,128)}) %reduce-scatter.2.cloned.1.call-update) | async-done | bytes 262160 | tf_op jit(solution)/shard_map/reduce_scatter | solution.py:40
  (4 shorter events, 0.0 us)
Async XLA Ops:
  7.2 1.0 copy-start
  42.6 190.6 %all-to-all-start = ((bf16[4,16,16,8192]{3,2,0,1:T(8,128)(2,1)}), bf16[4,16,16,8192]{3,2,0,1:T(8,128)(2,1)}, u32[]{:S(2)}, u32[]{:S(2)}) async-start(bf16[4,16,16,8192]{3,2,0,1:T(8,128)(2,1)} %copy.30), calls=%async_computation | async-start | bytes 33554432 | tf_op jit(solution)/shard_map/all_to_all | solution.py:24
  240.7 46.1 %copy-start.1 = (bf16[4,256,256]{2,1,0:T(8,128)(2,1)S(1)}, bf16[4,256,256]{2,1,0:T(8,128)(2,1)}, u32[]{:S(2)}) copy-start(bf16[4,256,256]{2,1,0:T(8,128)(2,1)} %param.7) | copy-start | bytes 1572868
  330.1 190.2 %all-to-all-start.1 = ((bf16[16,4,16,8192]{3,2,1,0:T(8,128)(2,1)}), bf16[16,4,16,8192]{3,2,1,0:T(8,128)(2,1)}, u32[]{:S(2)}, u32[]{:S(2)}) async-start(bf16[16,4,16,8192]{3,2,1,0:T(8,128)(2,1)} %copy.33), calls=%async_computation.1 | async-start | bytes 33554432 | tf_op jit(solution)/shard_map/all_to_all | solution.py:30
  337.2 264.4 %all-reduce.3.cloned.1.call-start = ((), (), s32[]{:S(2)}) async-start(), calls=%async_computation.4 | async-start | bytes 2097152
  548.5 82.6 %reduce-scatter.2.cloned.1.call-start = ((), (), s32[]{:S(2)}) async-start(), calls=%async_computation.3 | async-start | bytes 1310720 | tf_op jit(solution)/shard_map/reduce_scatter | solution.py:40
  548.6 14.8 %copy-start.2 = (u32[32]{0:T(128)S(1)}, u32[32]{0:T(128)}, u32[]{:S(2)}) copy-start(u32[32]{0:T(128)} %constant.8) | copy-start | bytes 388
Sparse Core Ops, SparseCore 0:
  548.6 52.9 all-reduce.2
  604.6 26.5 reduce-scatter.1
where the time goes:
time: 641 us; the launch traced here: 638 us
  waiting for transfers between devices  353 us (55%)
  local copies, waits for them, and re-layouts  156 us (24%)
  matrix products  85.4 us (13%)
  other arithmetic  15.3 us (2%)
  between operations  14.8 us (2%)
  starting transfers between devices  14.3 us (2%)
    all_to_all x1, waiting for transfers between devices, shards(): lax.all_to_all(masked, 'tensor', split_axis=0, concat_axis=1, tiled=True)  168 us
    all_to_all x1, waiting for transfers between devices, shards(): lax.all_to_all(hidden, 'tensor', split_axis=1, concat_axis=0, tiled=True)  156 us
    gt x2, local copies, waits for them, and re-layouts, shards(): moved > 0  46.1 us
    reshape x1, local copies, waits for them, and re-layouts, shards(): upstream = cotangent.reshape(tok_rows, blk_local, blk_width)  27.9 us
    reduce_scatter x1, waiting for transfers between devices, shards(): lax.psum_scatter(second_term, 'dp', scatter_dimension=1, tiled=True)  27.8 us
    unnamed x10, local copies, waits for them, and re-layouts  25.8 us
    dot_general x1, matrix products, shards(): jnp.einsum('tco,cjbo->bcjt', upstream, second_view, preferred_element_typ...  24.9 us
    dot_general x1, matrix products, shards(): jnp.einsum('tbi,bij->bjt', inputs, w_first, preferred_element_type=jnp.fl...  20.5 us
  transfers between devices with their start and end apart: 4, of which 4 were waited for; matrix products, arithmetic and copies ran while one was open for 15% of the time, Pallas kernels for 0%

commit v1 on v0

--- a/solution.py
+++ b/solution.py
@@ -5,6 +5,29 @@
 from jax.sharding import PartitionSpec as P
 
 NB = 16
+
+
+def _serve_node(point):
+    extra = lax.psum(1, "tensor")
+    v_next = lax.axis_index("tensor")
+    odd, step_out = (extra, v_next)
+    frame_out = point.shape[1] // odd
+    base_arr = list(point.shape)
+    base_arr[1] = frame_out
+    oldest = base_arr[0]
+    base_arr[0] = oldest * odd
+    all_values = jnp.zeros(base_arr, point.dtype)
+    for w in range(odd):
+        left_arr = lax.dynamic_slice_in_dim(point, (step_out ^ w) * frame_out, frame_out, axis=1)
+        if w:
+            f_next = range(odd)
+            part_next = map(lambda tick: (tick, tick ^ w), f_next)
+            big = list(part_next)
+            left_arr = lax.ppermute(left_arr, "tensor", big)
+        all_values = lax.dynamic_update_slice_in_dim(
+            all_values, left_arr, (step_out ^ w) * oldest, axis=0
+        )
+    return all_values
 
 
 def shards(tokens, cotangent, w_first, w_second):
@@ -21,7 +44,7 @@
     )
     hidden = hidden.reshape(blk_local, NB, sub_width, tok_rows)
     second_view = w_second.reshape(blk_local, sub_width, NB, blk_width)
-    moved = lax.all_to_all(hidden, "tensor", split_axis=1, concat_axis=0, tiled=True)
+    moved = _serve_node(hidden)
     active = jnp.maximum(moved, jnp.zeros((), jnp.bfloat16))
     second_term = jnp.einsum("bcjt,tco->cjbo", active, upstream, preferred_element_type=jnp.float32)
     second_term = second_term.reshape(blk_local, blk_width, blk_width) * grad_scale

time: 641 us -> 582 us (0.908)
  waiting for transfers between devices: 353 us -> 149 us
  blocking collectives: 0 us -> 186 us
  local copies, waits for them, and re-layouts: 156 us -> 135 us
  other arithmetic: 15.3 us -> 0 us
  starting transfers between devices: 14.3 us -> 3.14 us
    all_to_all x2 -> x0, waiting for transfers between devices: 324 us -> none  [the longest x1 168 us: shards(): lax.all_to_all(masked, 'tensor', split_axis=0, concat_axis=1, tiled=True)]
    all_to_all x0 -> x1, blocking collectives: none -> 186 us  [shards(): lax.all_to_all(masked, 'tensor', split_axis=0, concat_axis=1, tiled=True)]
    ppermute x0 -> x3, waiting for transfers between devices: none -> 121 us  [_serve_node(): left_arr = lax.ppermute(left_arr, 'tensor', big)]
    gt x2 -> x0, local copies, waits for them, and re-layouts: 46.1 us -> none  [shards(): moved > 0]
    dynamic_update_slice x0 -> x4, local copies, waits for them, and re-layouts: none -> 27.2 us  [_serve_node(): lax.dynamic_update_slice_in_dim(all_values, left_arr, (step_out ^ w) * ol...]
    unnamed x10 -> x15, local copies, waits for them, and re-layouts: 25.8 us -> 41.4 us
    all_to_all x2 -> x0, starting transfers between devices: 14.1 us -> none  [the longest x1 7.09 us: shards(): lax.all_to_all(masked, 'tensor', split_axis=0, concat_axis=1, tiled=True)]
    reshape x1 -> x0, local copies, waits for them, and re-layouts: 13.9 us -> none  [shards(): hidden = hidden.reshape(blk_local, NB, sub_width, tok_rows)]
  transfers between devices with their start and end apart: 4 -> 5, of which waited for: 4 -> 4; matrix products, arithmetic and copies ran while one was open for 15% -> 21% of each run, Pallas kernels for 0% -> 0%
where the time goes in v1:
time: 582 us; the launch traced here: 578 us
  blocking collectives  186 us (32%)
  waiting for transfers between devices  149 us (26%)
  local copies, waits for them, and re-layouts  135 us (23%)
  matrix products  89.7 us (15%)
  between operations  15 us (3%)
    all_to_all x1, blocking collectives, shards(): lax.all_to_all(masked, 'tensor', split_axis=0, concat_axis=1, tiled=True)  186 us
    ppermute x3, waiting for transfers between devices, _serve_node(): left_arr = lax.ppermute(left_arr, 'tensor', big)  121 us
    unnamed x15, local copies, waits for them, and re-layouts  41.4 us
    reshape x1, local copies, waits for them, and re-layouts, shards(): upstream = cotangent.reshape(tok_rows, blk_local, blk_width)  27.9 us
    reduce_scatter x1, waiting for transfers between devices, shards(): lax.psum_scatter(second_term, 'dp', scatter_dimension=1, tiled=True)  27.8 us
    dot_general x1, matrix products, shards(): jnp.einsum('tco,cjbo->bcjt', upstream, second_view, preferred_element_typ...  27.7 us
    dynamic_update_slice x4, local copies, waits for them, and re-layouts, _serve_node(): lax.dynamic_update_slice_in_dim(all_values, left_arr, (step_out ^ w) * ol...  27.2 us
    dot_general x1, matrix products, shards(): jnp.einsum('tbi,bij->bjt', inputs, w_first, preferred_element_type=jnp.fl...  20.6 us
  transfers between devices with their start and end apart: 5, of which 4 were waited for; matrix products, arithmetic and copies ran while one was open for 21% of the time, Pallas kernels for 0%

profile of v1, /device:TPU:0, one launch (start us, length us, event | category | flops | bytes accessed | tf_op | source)
XLA Modules:
  0.0 578.0 jit_solution(16631760199659432552)
XLA Ops:
  7.2 1.0 copy-done
  8.2 20.6 %fusion.7 = bf16[4,256,8192]{2,1,0:T(8,128)(2,1)} fusion(bf16[4,256,256]{2,1,0:T(8,128)(2,1)S(1)} %copy-done, bf16[1024,4,8,256]{3,2,1,0:T(8,128)(2,1)} %bitcast.43), kind=kOutput, calls=%fused_computation.8 | convolution fusion | flops 4303355904 | bytes 34078720 | tf_op jit(solution)/shard_map/tbi,bij->bjt/dot_general | solution.py:42
  28.8 8.8 %constant_dynamic-slice_fusion = (bf16[4,4,16,8192]{3,2,1,0:T(8,128)(2,1)S(1)}, bf16[4,4,16,8192]{3,2,1,0:T(8,128)(2,1)S(1)}, bf16[4,4,16,8192]{3,2,1,0:T(8,128)(2,1)S(1)}, bf16[4,4,16,8192]{3,2,1,0:T(8,128)(2,1)}) fusion(bf16[4,16,16,8192]{3,2,1,0:T(8,128)(2,1)} %bitcast.40, s32[]{:T(128)S(6)} %select_n.23, s32[]{:T(128)S(6)} %select_n.22, ...), kind=kLoop, calls=%fused_computation.20 | loop fusion | bytes 33554448 | tf_op jit(solution)/shard_map/dynamic_slice | solution.py:21
  37.7 5.2 copy.56
  42.9 0.5 collective-permute-start
  43.4 5.2 copy.57
  48.6 2.5 collective-permute-start.1
  51.0 5.2 copy.58
  56.3 0.1 collective-permute-start.2
  56.4 27.9 %reshape.31 = bf16[8192,4,256]{2,1,0:T(4,128)(2,1)} reshape(bf16[8192,1024]{1,0:T(8,128)(2,1)} %param.5) | data formatting | bytes 33554432 | tf_op jit(solution)/shard_map/reshape | solution.py:41
  84.3 7.2 %broadcast.13 = bf16[16,4,16,8192]{3,0,2,1:T(8,128)(2,1)} broadcast(bf16[]{:T(256)} %constant.2.clone.1), dimensions={} | broadcast | bytes 16777218 | tf_op jit(solution)/shard_map/broadcast.3
  91.5 5.3 copy_dynamic-update-slice_fusion
  96.7 7.3 %constant_dynamic-update-slice_fusion.2 = bf16[16,4,16,8192]{3,0,2,1:T(8,128)(2,1)} fusion(bf16[16,4,16,8192]{3,0,2,1:T(8,128)(2,1)} %copy_dynamic-update-slice_fusion, bf16[4,4,16,8192]{3,0,2,1:T(4,128)(2,1)} %collective-permute-done, s32[]{:T(128)S(6)} %select_n.21), kind=kLoop, calls=%fused_computation.23 | loop fusion | bytes 8388612 | tf_op jit(solution)/shard_map/dynamic_update_slice | solution.py:27
  104.1 38.7 %collective-permute-done.1 = bf16[4,4,16,8192]{3,0,2,1:T(4,128)(2,1)} collective-permute-done((bf16[4,4,16,8192]{3,0,2,1:T(4,128)(2,1)}, bf16[4,4,16,8192]{3,0,2,1:T(4,128)(2,1)}, u32[]{:S(2)}, u32[]{:S(2)}) %collective-permute-start.1) | collective-permute-done | bytes 4194336 | tf_op jit(solution)/shard_map/ppermute | solution.py:26
  142.8 7.3 %constant_dynamic-update-slice_fusion.1 = bf16[16,4,16,8192]{3,0,2,1:T(8,128)(2,1)} fusion(bf16[16,4,16,8192]{3,0,2,1:T(8,128)(2,1)} %constant_dynamic-update-slice_fusion.2, bf16[4,4,16,8192]{3,0,2,1:T(4,128)(2,1)} %collective-permute-done.1, s32[]{:T(128)S(6)} %select_n.22), kind=kLoop, calls=%fused_computation.21 | loop fusion | bytes 8388612 | tf_op jit(solution)/shard_map/dynamic_update_slice | solution.py:27
  150.1 82.2 %collective-permute-done.2 = bf16[4,4,16,8192]{3,0,2,1:T(4,128)(2,1)} collective-permute-done((bf16[4,4,16,8192]{3,0,2,1:T(4,128)(2,1)}, bf16[4,4,16,8192]{3,0,2,1:T(4,128)(2,1)}, u32[]{:S(2)}, u32[]{:S(2)}) %collective-permute-start.2) | collective-permute-done | bytes 4194336 | tf_op jit(solution)/shard_map/ppermute | solution.py:26
  232.3 7.3 %constant_dynamic-update-slice_fusion = bf16[16,4,16,8192]{3,0,2,1:T(8,128)(2,1)} fusion(bf16[16,4,16,8192]{3,0,2,1:T(8,128)(2,1)} %constant_dynamic-update-slice_fusion.1, bf16[4,4,16,8192]{3,0,2,1:T(4,128)(2,1)} %collective-permute-done.2, s32[]{:T(128)S(6)} %select_n.23), kind=kLoop, calls=%fused_computation.19 | loop fusion | bytes 8388612 | tf_op jit(solution)/shard_map/dynamic_update_slice | solution.py:27
  239.6 27.7 %fusion = bf16[16,4,16,8192]{3,0,2,1:T(8,128)(2,1)} fusion(bf16[16,4,16,8192]{3,0,2,1:T(8,128)(2,1)} %constant_dynamic-update-slice_fusion, bf16[4,16,16,256]{3,2,1,0:T(8,128)(2,1)S(1)} %bitcast.48, bf16[8192,4,256,1]{2,1,0,3:T(4,128)(2,1)} %bitcast.45), kind=kOutput, calls=%fused_computation.1 | convolution fusion | flops 4320133120 | bytes 50855936 | tf_op jit(solution)/shard_map/tco,cjbo->bcjt/dot_general | solution.py:51
  267.3 14.7 %copy.41 = bf16[16,4,16,8192]{3,2,1,0:T(8,128)(2,1)S(1)} copy(bf16[16,4,16,8192]{3,0,2,1:T(8,128)(2,1)} %fusion) | data formatting | bytes 33554432 | tf_op jit(solution)/shard_map/convert_element_type | solution.py:52
  282.0 186.1 %all_to_all.15 = bf16[16,4,16,8192]{3,2,1,0:T(8,128)(2,1)S(1)} all-to-all(bf16[16,4,16,8192]{3,2,1,0:T(8,128)(2,1)S(1)} %copy.41), channel_id=1, replica_groups=mesh['groups'=2,'tensor'=4,'dp'=4] {'tensor'}, dimensions={0} | all-to-all | bytes 33554432 | tf_op jit(solution)/shard_map/all_to_all | solution.py:53
  468.2 6.5 %copy.42 = bf16[4,4,4,16,8192]{4,3,2,0,1:T(8,128)(2,1)} copy(bf16[4,4,4,16,8192]{4,3,2,1,0:T(8,128)(2,1)S(1)} %bitcast.41) | data formatting | bytes 33554432 | tf_op jit(solution)/shard_map/all_to_all | solution.py:53
  474.7 12.9 %fusion.18 = f32[4,256,256]{1,2,0:T(8,128)S(1)} fusion(bf16[4,256,8192]{2,1,0:T(8,128)(2,1)} %bitcast.38, bf16[1024,4,8,256]{3,2,1,0:T(8,128)(2,1)} %bitcast.44), kind=kOutput, calls=%fused_computation.17 | convolution fusion | flops 4295229440 | bytes 34603008 | tf_op jit(solution)/shard_map/tbi,bjt->bij/dot_general | solution.py:56
  487.6 1.4 copy.44
  489.0 0.0 reduce-scatter.2.cloned.1.call-start
  489.1 14.5 %fusion.21 = f32[4,16,16,256]{3,1,2,0:T(8,128)} fusion(bf16[8192,4,256,1]{2,1,0,3:T(4,128)(2,1)} %bitcast.46, bf16[16,4,16,8192]{3,0,2,1:T(8,128)(2,1)} %constant_dynamic-update-slice_fusion), kind=kOutput, calls=%fused_computation.18 | convolution fusion | flops 4303618048 | bytes 34603008 | tf_op jit(solution)/shard_map/bcjt,tco->cjbo/dot_general | solution.py:49
  503.6 0.6 dynamic-slice
  504.9 13.9 %convolution_convert_fusion = bf16[4,8192,256]{1,2,0:T(8,128)(2,1)} fusion(bf16[4,256,256]{2,1,0:T(8,128)(2,1)S(1)} %copy-done, bf16[4,256,8192]{2,1,0:T(8,128)(2,1)} %bitcast.39), kind=kOutput, calls=%fused_computation.9 | convolution fusion | flops 4303355904 | bytes 34078720 | tf_op jit(solution)/shard_map/bjt,bij->tbi/dot_general | solution.py:59
  518.8 22.5 %copy.46 = bf16[8192,1024]{1,0:T(8,128)(2,1)} copy(bf16[8192,1024]{0,1:T(8,128)(2,1)} %bitcast.42) | data formatting | bytes 33554432
  541.3 0.1 all-reduce.3.cloned.1.call-done
  541.4 1.0 constant_dynamic-slice_fusion.4
  542.3 0.8 copy.47
  543.1 27.8 %reduce-scatter.2.cloned.1.call-done = f32[4,64,256]{2,1,0:T(8,128)} async-done(((f32[4,256,256]{2,1,0:T(8,128)}), f32[4,64,256]{2,1,0:T(8,128)}) %reduce-scatter.2.cloned.1.call-update) | async-done | bytes 262160 | tf_op jit(solution)/shard_map/reduce_scatter | solution.py:63
  (11 shorter events, 0.1 us)
Async XLA Ops:
  7.2 1.0 copy-start
  7.2 534.2 %all-reduce.3.cloned.1.call-start = ((), (), s32[]{:S(2)}) async-start(), calls=%async_computation.3 | async-start | bytes 2097152
  42.9 53.8 %collective-permute-start = (bf16[4,4,16,8192]{3,0,2,1:T(4,128)(2,1)}, bf16[4,4,16,8192]{3,0,2,1:T(4,128)(2,1)}, u32[]{:S(2)}, u32[]{:S(2)}) collective-permute-start(bf16[4,4,16,8192]{3,0,2,1:T(4,128)(2,1)} %copy.56), channel_id=1, source_target_pairs={{0,4},{4,0},{8,12},{12,8},{1,5},{5,1},{9,13},{13,9},{2,6},{6,2},{1... | collective-permute-start | bytes 12582920 | tf_op jit(solution)/shard_map/ppermute | solution.py:26
  48.6 94.2 %collective-permute-start.1 = (bf16[4,4,16,8192]{3,0,2,1:T(4,128)(2,1)}, bf16[4,4,16,8192]{3,0,2,1:T(4,128)(2,1)}, u32[]{:S(2)}, u32[]{:S(2)}) collective-permute-start(bf16[4,4,16,8192]{3,0,2,1:T(4,128)(2,1)} %copy.57), channel_id=1, source_target_pairs={{0,8},{4,12},{8,0},{12,4},{1,9},{5,13},{9,1},{13,5},{2,10},{6,14},... | collective-permute-start | bytes 12582920 | tf_op jit(solution)/shard_map/ppermute | solution.py:26
  56.3 176.0 %collective-permute-start.2 = (bf16[4,4,16,8192]{3,0,2,1:T(4,128)(2,1)}, bf16[4,4,16,8192]{3,0,2,1:T(4,128)(2,1)}, u32[]{:S(2)}, u32[]{:S(2)}) collective-permute-start(bf16[4,4,16,8192]{3,0,2,1:T(4,128)(2,1)} %copy.58), channel_id=1, source_target_pairs={{0,12},{4,8},{8,4},{12,0},{1,13},{5,9},{9,5},{13,1},{2,14},{6,10},... | collective-permute-start | bytes 12582920 | tf_op jit(solution)/shard_map/ppermute | solution.py:26
  84.3 7.2 %copy-start.1 = (bf16[4,4,16,8192]{3,2,1,0:T(8,128)(2,1)S(1)}, bf16[4,4,16,8192]{3,2,1,0:T(8,128)(2,1)}, u32[]{:S(2)}) copy-start(bf16[4,4,16,8192]{3,2,1,0:T(8,128)(2,1)} %get-tuple-element.15) | copy-start | bytes 12582916
  91.5 148.2 %copy-start.2 = (bf16[4,256,256]{2,1,0:T(8,128)(2,1)S(1)}, bf16[4,256,256]{2,1,0:T(8,128)(2,1)}, u32[]{:S(2)}) copy-start(bf16[4,256,256]{2,1,0:T(8,128)(2,1)} %param.7) | copy-start | bytes 1572868
  489.0 14.6 %copy-start.3 = (u32[32]{0:T(128)S(1)}, u32[32]{0:T(128)}, u32[]{:S(2)}) copy-start(u32[32]{0:T(128)} %constant.25) | copy-start | bytes 388
  489.0 81.9 %reduce-scatter.2.cloned.1.call-start = ((), (), s32[]{:S(2)}) async-start(), calls=%async_computation.2 | async-start | bytes 1310720 | tf_op jit(solution)/shard_map/reduce_scatter | solution.py:63
Sparse Core Ops, SparseCore 0:
  489.1 52.1 all-reduce.2
  544.3 26.5 reduce-scatter.1
